TPU v7x, 32 devices: a whole 2x2x4 slice. The times are simulated.
32 devices in a mesh: px: 4 (over y, x), py: 8 (over z, core).
Axes of the slice: x: 2, y: 2, z: 4, core: 2. Of those that a mesh axis runs over, the one named last changes fastest.
Arguments:
- residual: float32 [10, 2048, 2048], P(None, 'py', 'px'), may hold values from -6 to 6
- lambda_x: float32 [2048], P('px'), may hold values from 0.1 to 4
- lambda_y: float32 [2048], P('py'), may hold values from 0.1 to 4
- coupling: float32 [9], replicated, may hold values from 0.2 to 2
- layer_shift: float32 [10], replicated, may hold values from 0.05 to 1
- left_x: bfloat16 [2048, 2048], P(None, 'px'), may hold values from -0.125 to 0.125
- left_y: bfloat16 [2048, 2048], P('py'), may hold values from -0.125 to 0.125
- right_y: bfloat16 [2048, 2048], P('py'), may hold values from -0.125 to 0.125
- right_x: bfloat16 [2048, 2048], P(None, 'px'), may hold values from -0.125 to 0.125
- regime_code: int32 [10, 2048, 2048], P(None, 'py', 'px'), may hold values from 0 to 3
- upwind_flag: int32 [2, 10, 2048, 2048], P(None, None, 'py', 'px'), may hold values from 0 to 1
- mobility_table: float32 [4], replicated, may hold values from 0.3 to 3
Outputs:
- correction: float32 [10, 2048, 2048], P(None, 'py', 'px')
- balance: float32 [10, 2048, 2048], P(None, 'py', 'px')
Inputs may be any that keep to these rules, and one draw needn't show every extreme that they name: `regime_code`: a regime number of each cell.
All inputs are finite; a program needn't handle non-finite values.
Results may differ from a plain program's by a relative error of at most 0.0057.
Values may be sent and summed in bfloat16 or wider, within the bound.
No kernel may reach another device: no remote copies, remote signals or barrier semaphores. Data moves between devices by JAX's collectives and lax.ppermute only.
A program may use at most 192 MiB of HBM per device.

v0:
```python
import jax
import jax.numpy as jnp
from jax import lax
from jax.sharding import PartitionSpec as P


def with_halo(block, sides, width):
    for axis, dim in sides:
        count = lax.axis_size(axis)
        forward = [(i, i + 1) for i in range(count - 1)]
        backward = [(target, source) for source, target in forward]
        low = lax.ppermute(
            lax.slice_in_dim(block, block.shape[dim] - width, None, axis=dim), axis, forward
        )
        high = lax.ppermute(lax.slice_in_dim(block, 0, width, axis=dim), axis, backward)
        block = jnp.concatenate([low, block, high], axis=dim)
    return block


def thomas_solve(rhs, lambda_x, lambda_y, coupling, layer_shift):
    layers = rhs.shape[0]
    mode_sum = lambda_y[:, None] + lambda_x[None, :]
    ratios = []
    partial_values = []
    for layer_index in range(layers):
        diagonal = mode_sum + layer_shift[layer_index]
        if layer_index > 0:
            diagonal = diagonal + coupling[layer_index - 1]
        if layer_index < layers - 1:
            diagonal = diagonal + coupling[layer_index]
        if layer_index == 0:
            pivots = diagonal
            solved = rhs[0] / pivots
        else:
            pivots = diagonal + coupling[layer_index - 1] * ratios[-1]
            solved = (rhs[layer_index] + coupling[layer_index - 1] * partial_values[-1]) / pivots
        partial_values.append(solved)
        if layer_index < layers - 1:
            ratios.append(-coupling[layer_index] / pivots)
    results = [partial_values[layers - 1]]
    for layer_index in range(layers - 2, -1, -1):
        results.append(partial_values[layer_index] - ratios[layer_index] * results[-1])
    return jnp.stack(results[::-1])


def shards(
    residual,
    lambda_x,
    lambda_y,
    coupling,
    layer_shift,
    left_x,
    left_y,
    right_y,
    right_x,
    regime_code,
    upwind_flag,
    mobility_table,
):
    rounded = residual.astype(jnp.bfloat16)

    def forward(block):
        weights = left_x
        spectral_x = jnp.einsum(
            "zyx,xi->zyi",
            lax.all_gather(block, "px", axis=2, tiled=True),
            weights,
            preferred_element_type=jnp.float32,
        ).astype(jnp.bfloat16)
        weights = left_y
        return jnp.einsum(
            "jy,zyi->zji",
            weights,
            lax.all_gather(spectral_x, "py", axis=1, tiled=True),
            preferred_element_type=jnp.float32,
        )

    mobility = jnp.zeros(regime_code.shape, jnp.float32)
    for regime in range(mobility_table.shape[0]):
        mobility = jnp.where(regime_code == regime, mobility_table[regime], mobility)
    spectral = forward(rounded)
    solved = thomas_solve(spectral, lambda_x, lambda_y, coupling, layer_shift).astype(jnp.bfloat16)
    weights = right_y
    back_y = jnp.einsum(
        "yj,zji->zyi",
        weights,
        lax.all_gather(solved, "py", axis=1, tiled=True),
        preferred_element_type=jnp.float32,
    ).astype(jnp.bfloat16)
    weights = right_x
    correction = jnp.einsum(
        "zyi,ix->zyx",
        lax.all_gather(back_y, "px", axis=2, tiled=True),
        weights,
        preferred_element_type=jnp.float32,
    )
    width_x = correction.shape[2]
    width_y = correction.shape[1]
    stacked = jnp.stack(
        [
            correction,
            mobility,
            upwind_flag[0].astype(jnp.float32),
            upwind_flag[1].astype(jnp.float32),
        ]
    )
    extended = with_halo(stacked, (("px", 3), ("py", 2)), 1)
    press_x = extended[0][:, 1:-1, :]
    mobil_x = extended[1][:, 1:-1, :]
    flags_x = extended[2][:, 1:-1, :]
    upwind_x = jnp.where(flags_x[:, :, :-1] > 0.5, mobil_x[:, :, :-1], mobil_x[:, :, 1:])
    flux_x = upwind_x * (press_x[:, :, :-1] - press_x[:, :, 1:])
    faces_x = lax.axis_index("px") * width_x + jnp.arange(width_x + 1, dtype=jnp.int32)
    valid_x = (faces_x >= 1) & (faces_x <= width_x * lax.axis_size("px") - 1)
    flux_x = jnp.where(valid_x[None, None, :], flux_x, 0.0)
    net_x = flux_x[:, :, 1:] - flux_x[:, :, :-1]
    press_y = extended[0][:, :, 1:-1]
    mobil_y = extended[1][:, :, 1:-1]
    flags_y = extended[3][:, :, 1:-1]
    upwind_y = jnp.where(flags_y[:, :-1, :] > 0.5, mobil_y[:, :-1, :], mobil_y[:, 1:, :])
    flux_y = upwind_y * (press_y[:, :-1, :] - press_y[:, 1:, :])
    faces_y = lax.axis_index("py") * width_y + jnp.arange(width_y + 1, dtype=jnp.int32)
    valid_y = (faces_y >= 1) & (faces_y <= width_y * lax.axis_size("py") - 1)
    flux_y = jnp.where(valid_y[None, :, None], flux_y, 0.0)
    net_y = flux_y[:, 1:, :] - flux_y[:, :-1, :]
    balance = net_x + net_y
    return (correction, balance)


def solution(mesh):
    return jax.shard_map(
        shards,
        mesh=mesh,
        in_specs=(
            P(None, "py", "px"),
            P("px"),
            P("py"),
            P(),
            P(),
            P(None, "px"),
            P("py", None),
            P("py", None),
            P(None, "px"),
            P(None, "py", "px"),
            P(None, None, "py", "px"),
            P(),
        ),
        out_specs=(P(None, "py", "px"), P(None, "py", "px")),
        check_vma=False,
    )
```

profile of v0, /device:TPU:3, one launch (start us, length us, event | category | flops | bytes accessed | tf_op | source)
XLA Modules:
  0.0 841.1 jit_solution(6633718282841774213)
XLA Ops:
  7.2 0.0 all-gather.5.cloned.1.call-start
  7.2 4.5 convert_element_type.21
  11.7 0.0 all-gather.5.cloned.1.call-update
  11.8 0.0 all-gather.7.cloned.1.call-start
  11.8 106.2 %all-gather.5.cloned.1.call-done = bf16[10,256,2048]{2,1,0:T(8,128)(2,1)} async-done(((bf16[10,256,512]{2,1,0:T(8,128)(2,1)}), bf16[10,256,2048]{2,1,0:T(8,128)(2,1)}) %all-gather.5.cloned.1.call-update) | async-done | bytes 10485776 | tf_op jit(solution)/shard_map/all_gather | solution.py:66
  118.0 9.4 %fusion.9 = bf16[10,256,512]{1,2,0:T(8,128)(2,1)} fusion(bf16[10,256,2048]{2,1,0:T(8,128)(2,1)} %all-gather.5.cloned.1.call-done, bf16[2048,512]{1,0:T(8,128)(2,1)S(1)} %copy-done), kind=kOutput, calls=%fused_computation.41 | convolution fusion | flops 5370019840 | bytes 15204352 | tf_op jit(solution)/shard_map/zyx,xi->zyi/dot_general | solution.py:64
  127.5 0.5 all-gather.9.cloned.1.call-start
  128.0 0.7 fusion.71
  134.2 0.7 fusion.70
  134.9 179.7 %all-gather.7.cloned.1.call-done = bf16[10,2048,512]{1,2,0:T(8,128)(2,1)} async-done(((bf16[10,256,512]{1,2,0:T(8,128)(2,1)}), bf16[10,2048,512]{1,2,0:T(8,128)(2,1)}) %all-gather.7.cloned.1.call-update) | async-done | bytes 20971536 | tf_op jit(solution)/shard_map/all_gather | solution.py:74
  314.6 10.3 %convolution_bitcast_fusion = f32[10,256,512]{1,2,0:T(8,128)S(1)} fusion(bf16[10,2048,512]{1,2,0:T(8,128)(2,1)} %all-gather.7.cloned.1.call-done, bf16[256,2048]{1,0:T(8,128)(2,1)S(1)} %copy-done.16), kind=kOutput, calls=%fused_computation.36 | convolution fusion | flops 5368709120 | bytes 27262976 | tf_op jit(solution)/shard_map/jy,zyi->zji/dot_general | solution.py:71
  324.9 14.8 %fusion.59 = (bf16[10,256,512]{1,2,0:T(8,128)(2,1)}, bf16[1,256,512]{1,2,0:T(8,128)(2,1)S(1)}, f32[1,256,512]{1,2,0:T(8,128)S(1)}, f32[1,256,512]{1,2,0:T(8,128)...) fusion(f32[]{:T(128)S(6)} %neg.27, f32[]{:T(128)} %bitcast.4, ...), kind=kLoop, calls=%fused_computation.107 | loop fusion | flops 13631487 | bytes 8916080
  339.7 0.7 convert_dynamic-update-slice_fusion.8
  340.4 4.8 convert_dynamic-update-slice_fusion.7
  345.2 0.7 convert_dynamic-update-slice_fusion.6
  345.9 7.5 convert_dynamic-update-slice_fusion.5
  353.4 0.7 convert_dynamic-update-slice_fusion.4
  354.1 10.2 %convert_dynamic-update-slice_fusion.3 = bf16[10,256,512]{1,2,0:T(8,128)(2,1)} fusion(bf16[10,256,512]{1,2,0:T(8,128)(2,1)} %convert_dynamic-update-slice_fusion.4, f32[1,256,512]{1,2,0:T(8,128)S(1)} %get-tuple-element.7, f32[1,256,512]{1,2,0:T(8,128)S(1)} %get-tuple-element.6, f32[]{:T(128)} %bitcast.3, f32[]{:T(128)S(6)} %neg.27, f32[]{:T(128)} %bitcast.4, ...), kind=kLoop, calls=%fused_computation.111 | loop fusion | flops 5636096 | bytes 1320988
  364.3 0.7 convert_dynamic-update-slice_fusion.2
  365.1 13.9 %convert_dynamic-update-slice_fusion.1 = bf16[10,256,512]{1,2,0:T(8,128)(2,1)} fusion(bf16[10,256,512]{1,2,0:T(8,128)(2,1)} %convert_dynamic-update-slice_fusion.2, f32[]{:T(128)} %bitcast.3, f32[]{:T(128)S(6)} %neg.27, f32[]{:T(128)} %bitcast.4, f32[]{:T(128)} %bitcast.5, f32[]{:T(128)S(6)} %neg.28, f32[]{:T(128)} %bitcast.6, f32[]{:T(128)} %bitcast.7, ...), kind=kLoop, calls=%fused_computation.109 | loop fusion | flops 8912896 | bytes 2372132
  379.0 13.9 %convert_dynamic-update-slice_fusion = bf16[10,256,512]{1,2,0:T(8,128)(2,1)} fusion(bf16[10,256,512]{1,2,0:T(8,128)(2,1)} %convert_dynamic-update-slice_fusion.1, f32[]{:T(128)} %bitcast.3, f32[]{:T(128)S(6)} %neg.27, f32[]{:T(128)} %bitcast.4, f32[]{:T(128)} %bitcast.5, f32[]{:T(128)S(6)} %neg.28, f32[]{:T(128)} %bitcast.6, f32[]{:T(128)} %bitcast.7, ...), kind=kLoop, calls=%fused_computation.108 | loop fusion | flops 8650752 | bytes 2372132 | tf_op jit(solution)/shard_map/stack | solution.py:43
  392.9 0.2 all-gather.11.cloned.1.call-start
  393.1 184.6 %all-gather.9.cloned.1.call-done = bf16[10,2048,512]{1,2,0:T(8,128)(2,1)} async-done(((bf16[10,256,512]{1,2,0:T(8,128)(2,1)}), bf16[10,2048,512]{1,2,0:T(8,128)(2,1)}) %all-gather.9.cloned.1.call-update) | async-done | bytes 20971536 | tf_op jit(solution)/shard_map/all_gather | solution.py:87
  577.7 22.0 %convert_bitcast_fusion = bf16[10,256,512]{2,1,0:T(8,128)(2,1)} fusion(bf16[10,2048,512]{1,2,0:T(8,128)(2,1)} %all-gather.9.cloned.1.call-done, bf16[256,2048]{1,0:T(8,128)(2,1)S(1)} %copy-done.17), kind=kOutput, calls=%fused_computation.25 | convolution fusion | flops 5370019840 | bytes 24641536 | tf_op jit(solution)/shard_map/yj,zji->zyi/dot_general | solution.py:84
  599.8 0.7 fusion.69
  600.5 9.1 %select_bitcast_fusion = f32[1,10,256,512]{3,2,1,0:T(8,128)} fusion(s32[10,256,512]{2,1,0:T(8,128)} %param.21, f32[]{:T(128)} %bitcast.29, f32[]{:T(128)} %bitcast.28, f32[]{:T(128)} %bitcast.27, f32[]{:T(128)} %bitcast.26), kind=kLoop, calls=%fused_computation.24 | loop fusion | flops 10485760 | bytes 10485776 | tf_op jit(solution)/shard_map/stack | solution.py:99
  609.6 10.4 %slice_convert_fusion.1 = (f32[1,10,256,512]{3,2,1,0:T(8,128)}, f32[1,10,256,512]{3,2,1,0:T(8,128)}) fusion(s32[2,10,256,512]{3,2,1,0:T(8,128)} %param.22), kind=kLoop, calls=%fused_computation.23 | loop fusion | flops 2621440 | bytes 20971520 | tf_op jit(solution)/shard_map/convert_element_type | solution.py:103
  620.0 82.6 %all-gather.11.cloned.1.call-done = bf16[10,256,2048]{2,1,0:T(8,128)(2,1)} async-done(((bf16[10,256,512]{2,1,0:T(8,128)(2,1)}), bf16[10,256,2048]{2,1,0:T(8,128)(2,1)}) %all-gather.11.cloned.1.call-update) | async-done | bytes 10485776 | tf_op jit(solution)/shard_map/all_gather | solution.py:93
  702.6 8.5 %fusion.5 = f32[10,256,512]{2,1,0:T(8,128)S(1)} fusion(bf16[10,256,2048]{2,1,0:T(8,128)(2,1)} %all-gather.11.cloned.1.call-done, bf16[2048,512]{1,0:T(8,128)(2,1)S(1)} %copy-done.15), kind=kOutput, calls=%fused_computation.37 | convolution fusion | flops 5368709120 | bytes 17825792 | tf_op jit(solution)/shard_map/zyi,ix->zyx/dot_general | solution.py:91
  711.1 0.1 copy-done.6
  711.2 5.9 pad_maximum_fusion.4
  717.1 3.3 copy.14
  720.4 3.1 collective-permute-start
  723.5 3.3 copy.15
  726.8 2.2 collective-permute-start.1
  729.0 3.2 copy.16
  732.2 0.3 collective-permute-done.1
  732.5 3.1 copy.17
  735.6 2.3 pad_maximum_fusion.10
  737.9 5.4 collective-permute-start.2
  743.3 2.1 collective-permute-start.3
  745.4 3.8 collective-permute-done.3
  749.3 27.6 %pad_maximum_fusion = f32[4,10,258,514]{3,2,1,0:T(8,128)} fusion(f32[4,10,1,514]{3,2,1,0:T(1,128)S(1)} %collective-permute-done.3, f32[4,10,256,1]{3,2,1,0:T(8,128)S(1)} %copy-done.8, f32[1,10,256,512]{3,2,1,0:T(8,128)} %get-tuple-element.19, f32[1,10,256,512]{3,2,1,0:T(8,128)S(1)} %bitcast.57, f32[1,10,256,512]{3,2,1,0:T(8,128)} %select_bitcast_fusion, ...), kind=kLoop, calls=%fused_computation | loop fusion | flops 37131360 | bytes 42435840 | tf_op jit(solution)/shard_map/concatenate | solution.py:16
  776.9 18.6 %slice_bitcast_fusion.3 = (f32[10,258,514]{2,1,0:T(8,128)}, f32[10,258,514]{2,1,0:T(8,128)}, f32[10,258,514]{2,1,0:T(8,128)}, f32[10,258,514]{2,1,0:T(8,128)}) fusion(f32[4,10,258,514]{3,2,1,0:T(8,128)} %pad_maximum_fusion), kind=kLoop, calls=%fused_computation.4 | loop fusion | bytes 42435840 | tf_op jit(solution)/shard_map/squeeze | solution.py:110
  795.5 14.9 %fusion.1 = f32[10,256,513]{2,1,0:T(8,128)} fusion(f32[10,258,514]{2,1,0:T(8,128)} %get-tuple-element.14, f32[10,258,514]{2,1,0:T(8,128)} %get-tuple-element.15, f32[10,258,514]{2,1,0:T(8,128)} %get-tuple-element.12, pred[513]{0:T(1024)(128)(4,1)S(1)} %fusion.62), kind=kLoop, calls=%fused_computation.7 | loop fusion | flops 6566400 | bytes 31519232 | tf_op jit(solution)/shard_map/jit(_where)/select_n | solution.py:115
  810.4 1.9 copy-done.3
  812.3 10.7 %fusion.3 = f32[10,257,512]{2,1,0:T(8,128)} fusion(f32[10,258,514]{2,1,0:T(8,128)S(1)} %copy-done.2, f32[10,258,514]{2,1,0:T(8,128)S(1)} %copy-done.3, f32[10,258,514]{2,1,0:T(8,128)} %get-tuple-element.13, pred[257]{0:T(512)(128)(4,1)S(1)} %fusion.65), kind=kLoop, calls=%fused_computation.12 | loop fusion | flops 6579200 | bytes 31580416 | tf_op jit(solution)/shard_map/jit(_where)/select_n | solution.py:124
  823.1 11.2 %fusion.4 = f32[10,256,512]{2,1,0:T(8,128)} fusion(f32[10,257,512]{2,1,0:T(8,128)} %fusion.3, f32[10,256,513]{2,1,0:T(8,128)} %fusion.1), kind=kLoop, calls=%fused_computation.16 | loop fusion | flops 3932160 | bytes 26214400 | tf_op jit(solution)/shard_map/add | solution.py:126
  (46 shorter events, 0.2 us)
Async XLA Ops:
  7.2 110.8 %copy-start = (bf16[2048,512]{1,0:T(8,128)(2,1)S(1)}, bf16[2048,512]{1,0:T(8,128)(2,1)}, u32[]{:S(2)}) copy-start(bf16[2048,512]{1,0:T(8,128)(2,1)} %param.17) | copy-start | bytes 6291460
  7.2 110.8 %all-gather.5.cloned.1.call-start = ((), (), s32[]{:S(2)}) async-start(), calls=%async_computation | async-start | bytes 13107200 | tf_op jit(solution)/shard_map/all_gather | solution.py:66
  11.7 116.3 %copy-start.12 = (f32[9]{0:T(128)S(1)}, f32[9]{0:T(128)}, u32[]{:S(2)}) copy-start(f32[9]{0:T(128)} %param.15) | copy-start | bytes 112
  11.7 122.4 %copy-start.11 = (f32[10]{0:T(128)S(1)}, f32[10]{0:T(128)}, u32[]{:S(2)}) copy-start(f32[10]{0:T(128)} %param.16) | copy-start | bytes 124
  11.8 302.8 %copy-start.16 = (bf16[256,2048]{1,0:T(8,128)(2,1)S(1)}, bf16[256,2048]{1,0:T(8,128)(2,1)}, u32[]{:S(2)}) copy-start(bf16[256,2048]{1,0:T(8,128)(2,1)} %param.18) | copy-start | bytes 3145732
  11.8 302.8 %all-gather.7.cloned.1.call-start = ((), (), s32[]{:S(2)}) async-start(), calls=%async_computation.1 | async-start | bytes 23592960 | tf_op jit(solution)/shard_map/all_gather | solution.py:74
  127.5 450.3 %all-gather.9.cloned.1.call-start = ((), (), s32[]{:S(2)}) async-start(), calls=%async_computation.2 | async-start | bytes 23592960 | tf_op jit(solution)/shard_map/all_gather | solution.py:87
  134.9 190.0 %copy-start.10 = (f32[512]{0:T(512)S(1)}, f32[512]{0:T(512)}, u32[]{:S(2)}) copy-start(f32[512]{0:T(512)} %param.13) | copy-start | bytes 6148
  134.9 190.0 %copy-start.13 = (f32[256]{0:T(256)S(1)}, f32[256]{0:T(256)}, u32[]{:S(2)}) copy-start(f32[256]{0:T(256)} %param.14) | copy-start | bytes 3076
  353.4 224.4 %copy-start.17 = (bf16[256,2048]{1,0:T(8,128)(2,1)S(1)}, bf16[256,2048]{1,0:T(8,128)(2,1)}, u32[]{:S(2)}) copy-start(bf16[256,2048]{1,0:T(8,128)(2,1)} %param.19) | copy-start | bytes 3145732
  392.9 206.9 %copy-start.14 = (f32[4]{0:T(128)S(1)}, f32[4]{0:T(128)}, u32[]{:S(2)}) copy-start(f32[4]{0:T(128)} %param.23) | copy-start | bytes 52
  392.9 309.7 %all-gather.11.cloned.1.call-start = ((), (), s32[]{:S(2)}) async-start(), calls=%async_computation.3 | async-start | bytes 13107200 | tf_op jit(solution)/shard_map/all_gather | solution.py:93
  609.6 93.0 %copy-start.15 = (bf16[2048,512]{1,0:T(8,128)(2,1)S(1)}, bf16[2048,512]{1,0:T(8,128)(2,1)}, u32[]{:S(2)}) copy-start(bf16[2048,512]{1,0:T(8,128)(2,1)} %param.20) | copy-start | bytes 6291460
  702.6 8.5 %copy-start.4 = (f32[1,10,256,512]{3,2,1,0:T(8,128)S(1)}, f32[1,10,256,512]{3,2,1,0:T(8,128)}, u32[]{:S(2)}) copy-start(f32[1,10,256,512]{3,2,1,0:T(8,128)} %get-tuple-element.18) | copy-start | bytes 15728644
  702.6 8.5 %copy-start.5 = (f32[1,10,256,512]{3,2,1,0:T(8,128)S(1)}, f32[1,10,256,512]{3,2,1,0:T(8,128)}, u32[]{:S(2)}) copy-start(f32[1,10,256,512]{3,2,1,0:T(8,128)} %get-tuple-element.19) | copy-start | bytes 15728644
  702.6 8.6 %copy-start.6 = (f32[1,10,256,512]{3,2,1,0:T(8,128)S(1)}, f32[1,10,256,512]{3,2,1,0:T(8,128)}, u32[]{:S(2)}) copy-start(f32[1,10,256,512]{3,2,1,0:T(8,128)} %select_bitcast_fusion) | copy-start | bytes 15728644
  711.1 6.0 copy-start.9
  720.4 8.6 %collective-permute-start = (f32[4,10,256,1]{2,0,3,1:T(4,128)S(1)}, f32[4,10,256,1]{2,0,3,1:T(4,128)S(1)}, u32[]{:S(2)}, u32[]{:S(2)}) collective-permute-start(f32[4,10,256,1]{2,0,3,1:T(4,128)S(1)} %copy.14), channel_id=1, source_target_pairs={{0,8},{8,16},{16,24},{1,9},{9,17},{17,25},{2,10},{10,18},{18,26},{... | collective-permute-start | bytes 122888 | tf_op jit(solution)/shard_map/ppermute | solution.py:12
  726.8 5.6 collective-permute-start.1
  732.5 16.8 %slice-start = ((s8[5242880]{0:T(1024)(128)(4,1)}), s8[1048576]{0:T(1024)(128)(4,1)S(1)}, s32[]{:S(2)}) async-start(s8[5242880]{0:T(1024)(128)(4,1)} %bitcast.56), calls=%async_computation.4 | async-start | bytes 2097152
  735.6 13.7 %slice-start.1 = ((s8[5242880]{0:T(1024)(128)(4,1)}), s8[4194304]{0:T(1024)(128)(4,1)S(1)}, s32[]{:S(2)}) async-start(s8[5242880]{0:T(1024)(128)(4,1)} %bitcast.56), calls=%async_computation.5 | async-start | bytes 8388608
  735.6 13.7 %copy-start.7 = (f32[4,10,256,1]{3,2,1,0:T(8,128)S(1)}, f32[4,10,256,1]{3,2,1,0:T(8,128)}, u32[]{:S(2)}) copy-start(f32[4,10,256,1]{3,2,1,0:T(8,128)} %copy.16) | copy-start | bytes 122884
  735.6 13.7 %copy-start.8 = (f32[4,10,256,1]{3,2,1,0:T(8,128)S(1)}, f32[4,10,256,1]{3,2,1,0:T(8,128)}, u32[]{:S(2)}) copy-start(f32[4,10,256,1]{3,2,1,0:T(8,128)} %copy.17) | copy-start | bytes 122884
  737.9 7.5 collective-permute-start.2
  743.3 6.0 collective-permute-start.3
  795.5 14.9 %copy-start.2 = (f32[10,258,514]{2,1,0:T(8,128)S(1)}, f32[10,258,514]{2,1,0:T(8,128)}, u32[]{:S(2)}) copy-start(f32[10,258,514]{2,1,0:T(8,128)} %get-tuple-element.14) | copy-start | bytes 15913444
  795.5 16.9 %copy-start.3 = (f32[10,258,514]{2,1,0:T(8,128)S(1)}, f32[10,258,514]{2,1,0:T(8,128)}, u32[]{:S(2)}) copy-start(f32[10,258,514]{2,1,0:T(8,128)} %get-tuple-element.15) | copy-start | bytes 15913444
  823.1 11.2 %copy-start.1 = (bf16[2048,512]{1,0:T(8,128)(2,1)S(1)}, bf16[2048,512]{1,0:T(8,128)(2,1)}, u32[]{:S(2)}) copy-start(bf16[2048,512]{1,0:T(8,128)(2,1)} %param.17) | copy-start | bytes 6291460
Sparse Core Ops, SparseCore 0:
  11.9 106.1 all-gather.4
  127.6 186.9 all-gather.6
  393.0 184.6 all-gather.8
  599.9 102.6 all-gather.10
where the time goes:
time: 845 us; the launch traced here: 841 us
  waiting for transfers between devices  557 us (66%)
  other arithmetic  164 us (19%)
  matrix products  50.2 us (6%)
  local copies, waits for them, and re-layouts  36.2 us (4%)
  between operations  19.7 us (2%)
  starting transfers between devices  13.6 us (2%)
    all_gather x1, waiting for transfers between devices, shards(): lax.all_gather(solved, 'py', axis=1, tiled=True)  185 us
    all_gather x1, waiting for transfers between devices, forward(): lax.all_gather(spectral_x, 'py', axis=1, tiled=True)  180 us
    all_gather x1, waiting for transfers between devices, forward(): lax.all_gather(block, 'px', axis=2, tiled=True)  106 us
    all_gather x1, waiting for transfers between devices, shards(): lax.all_gather(back_y, 'px', axis=2, tiled=True)  82.6 us
    unnamed x9, other arithmetic  53.4 us
    concatenate x1, other arithmetic, with_halo(): block = jnp.concatenate([low, block, high], axis=dim)  27.6 us
    dot_general x1, matrix products, shards(): jnp.einsum('yj,zji->zyi', weights, lax.all_gather(solved, 'py', axis=1, t...  22 us
    squeeze x1, local copies, waits for them, and re-layouts, shards(): flags_x = extended[2][:, 1:-1, :]  18.6 us
  transfers between devices with their start and end apart: 8, of which 6 were waited for; matrix products, arithmetic and copies ran while one was open for 3% of the time, Pallas kernels for 0%

commit v1 on v0

--- a/solution.py
+++ b/solution.py
@@ -2,6 +2,24 @@
 import jax.numpy as jnp
 from jax import lax
 from jax.sharding import PartitionSpec as P
+
+
+def collect(value, axis, dim):
+    ways, here, step = (lax.axis_size(axis), lax.axis_index(axis), value.shape[dim])
+    dims = [n * ways if d == dim else n for d, n in enumerate(value.shape)]
+    full = lax.dynamic_update_slice_in_dim(
+        jnp.zeros(dims, value.dtype), value, here * step, axis=dim
+    )
+    going_up = going_down = value
+    for far in range(1, ways // 2 + 1):
+        going_up = lax.ppermute(going_up, axis, [(d, (d + 1) % ways) for d in range(ways)])
+        full = lax.dynamic_update_slice_in_dim(full, going_up, (here - far) % ways * step, axis=dim)
+        if 2 * far < ways:
+            going_down = lax.ppermute(going_down, axis, [(d, (d - 1) % ways) for d in range(ways)])
+            full = lax.dynamic_update_slice_in_dim(
+                full, going_down, (here + far) % ways * step, axis=dim
+            )
+    return full
 
 
 def with_halo(block, sides, width):
@@ -89,10 +107,7 @@
     ).astype(jnp.bfloat16)
     weights = right_x
     correction = jnp.einsum(
-        "zyi,ix->zyx",
-        lax.all_gather(back_y, "px", axis=2, tiled=True),
-        weights,
-        preferred_element_type=jnp.float32,
+        "zyi,ix->zyx", collect(back_y, "px", 2), weights, preferred_element_type=jnp.float32
     )
     width_x = correction.shape[2]
     width_y = correction.shape[1]

time: 845 us -> 913 us (1.080)
  waiting for transfers between devices: 557 us -> 596 us
  local copies, waits for them, and re-layouts: 36.2 us -> 70.2 us
  matrix products: 50.2 us -> 41 us
    ppermute x0 -> x3, waiting for transfers between devices: none -> 122 us  [the longest x2 102 us: collect(): lax.ppermute(going_up, axis, [(d, (d + 1) % ways) for d in range(ways)])]
    all_gather x1 -> x0, waiting for transfers between devices: 82.6 us -> none  [shards(): lax.all_gather(back_y, 'px', axis=2, tiled=True)]
    ppermute x0 -> x3, local copies, waits for them, and re-layouts: none -> 13.2 us  [the longest x2 8.8 us: collect(): lax.ppermute(going_up, axis, [(d, (d + 1) % ways) for d in range(ways)])]
    dynamic_update_slice x0 -> x4, local copies, waits for them, and re-layouts: none -> 11 us  [the longest x2 7.39 us: collect(): lax.dynamic_update_slice_in_dim(full, going_up, (here - far) % ways * ste...]
    dot_general x1, matrix products: 22 us -> 12.1 us  [shards(): jnp.einsum('yj,zji->zyi', weights, lax.all_gather(solved, 'py', axis=1, t...]
    unnamed x9 -> x12, other arithmetic: 53.4 us -> 54.1 us
  transfers between devices with their start and end apart: 8 -> 10, of which waited for: 6 -> 8; matrix products, arithmetic and copies ran while one was open for 3% -> 6% of each run, Pallas kernels for 0% -> 0%
where the time goes in v1:
time: 913 us; the launch traced here: 908 us
  waiting for transfers between devices  596 us (65%)
  other arithmetic  164 us (18%)
  local copies, waits for them, and re-layouts  70.2 us (8%)
  matrix products  41 us (4%)
  between operations  20 us (2%)
  starting transfers between devices  16.1 us (2%)
    all_gather x1, waiting for transfers between devices, shards(): lax.all_gather(solved, 'py', axis=1, tiled=True)  185 us
    all_gather x1, waiting for transfers between devices, forward(): lax.all_gather(spectral_x, 'py', axis=1, tiled=True)  180 us
    all_gather x1, waiting for transfers between devices, forward(): lax.all_gather(block, 'px', axis=2, tiled=True)  106 us
    ppermute x2, waiting for transfers between devices, collect(): lax.ppermute(going_up, axis, [(d, (d + 1) % ways) for d in range(ways)])  102 us
    unnamed x12, other arithmetic  54.1 us
    concatenate x1, other arithmetic, with_halo(): block = jnp.concatenate([low, block, high], axis=dim)  27.8 us
    ppermute x1, waiting for transfers between devices, collect(): lax.ppermute(going_down, axis, [(d, (d - 1) % ways) for d in range(ways)])  19.6 us
    squeeze x1, local copies, waits for them, and re-layouts, shards(): flags_x = extended[2][:, 1:-1, :]  18.6 us
  transfers between devices with their start and end apart: 10, of which 8 were waited for; matrix products, arithmetic and copies ran while one was open for 6% of the time, Pallas kernels for 0%

profile of v1, /device:TPU:3, one launch (start us, length us, event | category | flops | bytes accessed | tf_op | source)
XLA Modules:
  0.0 907.7 jit_solution(17692682190680909840)
XLA Ops:
  7.2 4.5 convert_element_type.21
  11.8 106.2 %all-gather.4.cloned.1.call-done = bf16[10,256,2048]{2,1,0:T(8,128)(2,1)} async-done(((bf16[10,256,512]{2,1,0:T(8,128)(2,1)}), bf16[10,256,2048]{2,1,0:T(8,128)(2,1)}) %all-gather.4.cloned.1.call-update) | async-done | bytes 10485776 | tf_op jit(solution)/shard_map/all_gather | solution.py:84
  118.0 9.4 %fusion.9 = bf16[10,256,512]{1,2,0:T(8,128)(2,1)} fusion(bf16[10,256,2048]{2,1,0:T(8,128)(2,1)} %all-gather.4.cloned.1.call-done, bf16[2048,512]{1,0:T(8,128)(2,1)S(1)} %copy-done), kind=kOutput, calls=%fused_computation.41 | convolution fusion | flops 5370019840 | bytes 15204352 | tf_op jit(solution)/shard_map/zyx,xi->zyi/dot_general | solution.py:82
  134.9 179.7 %all-gather.6.cloned.1.call-done = bf16[10,2048,512]{1,2,0:T(8,128)(2,1)} async-done(((bf16[10,256,512]{1,2,0:T(8,128)(2,1)}), bf16[10,2048,512]{1,2,0:T(8,128)(2,1)}) %all-gather.6.cloned.1.call-update) | async-done | bytes 20971536 | tf_op jit(solution)/shard_map/all_gather | solution.py:92
  314.6 10.3 %convolution_bitcast_fusion = f32[10,256,512]{1,2,0:T(8,128)S(1)} fusion(bf16[10,2048,512]{1,2,0:T(8,128)(2,1)} %all-gather.6.cloned.1.call-done, bf16[256,2048]{1,0:T(8,128)(2,1)S(1)} %copy-done.15), kind=kOutput, calls=%fused_computation.36 | convolution fusion | flops 5368709120 | bytes 27262976 | tf_op jit(solution)/shard_map/jy,zyi->zji/dot_general | solution.py:89
  324.9 14.9 %fusion.59 = (bf16[10,256,512]{1,2,0:T(8,128)(2,1)}, bf16[1,256,512]{1,2,0:T(8,128)(2,1)S(1)}, f32[1,256,512]{1,2,0:T(8,128)S(1)}, f32[1,256,512]{1,2,0:T(8,128)...) fusion(f32[]{:T(128)S(6)} %neg.27, f32[]{:T(128)} %bitcast.4, ...), kind=kLoop, calls=%fused_computation.107 | loop fusion | flops 13631487 | bytes 8916080
  340.6 4.9 convert_dynamic-update-slice_fusion.7
  346.2 7.7 convert_dynamic-update-slice_fusion.5
  354.6 10.4 %convert_dynamic-update-slice_fusion.3 = bf16[10,256,512]{1,2,0:T(8,128)(2,1)} fusion(bf16[10,256,512]{1,2,0:T(8,128)(2,1)} %convert_dynamic-update-slice_fusion.4, f32[1,256,512]{1,2,0:T(8,128)S(1)} %get-tuple-element.7, f32[1,256,512]{1,2,0:T(8,128)S(1)} %get-tuple-element.6, f32[]{:T(128)} %bitcast.3, f32[]{:T(128)S(6)} %neg.27, f32[]{:T(128)} %bitcast.4, ...), kind=kLoop, calls=%fused_computation.111 | loop fusion | flops 5636096 | bytes 1320988
  365.0 0.7 convert_dynamic-update-slice_fusion.2
  365.7 14.0 %convert_dynamic-update-slice_fusion.1 = bf16[10,256,512]{1,2,0:T(8,128)(2,1)} fusion(bf16[10,256,512]{1,2,0:T(8,128)(2,1)} %convert_dynamic-update-slice_fusion.2, f32[]{:T(128)} %bitcast.3, f32[]{:T(128)S(6)} %neg.27, f32[]{:T(128)} %bitcast.4, f32[]{:T(128)} %bitcast.5, f32[]{:T(128)S(6)} %neg.28, f32[]{:T(128)} %bitcast.6, f32[]{:T(128)} %bitcast.7, ...), kind=kLoop, calls=%fused_computation.109 | loop fusion | flops 8912896 | bytes 2372132
  379.7 14.0 %convert_dynamic-update-slice_fusion = bf16[10,256,512]{1,2,0:T(8,128)(2,1)} fusion(bf16[10,256,512]{1,2,0:T(8,128)(2,1)} %convert_dynamic-update-slice_fusion.1, f32[]{:T(128)} %bitcast.3, f32[]{:T(128)S(6)} %neg.27, f32[]{:T(128)} %bitcast.4, f32[]{:T(128)} %bitcast.5, f32[]{:T(128)S(6)} %neg.28, f32[]{:T(128)} %bitcast.6, f32[]{:T(128)} %bitcast.7, ...), kind=kLoop, calls=%fused_computation.108 | loop fusion | flops 8650752 | bytes 2372132 | tf_op jit(solution)/shard_map/stack | solution.py:61
  393.8 184.8 %all-gather.8.cloned.1.call-done = bf16[10,2048,512]{1,2,0:T(8,128)(2,1)} async-done(((bf16[10,256,512]{1,2,0:T(8,128)(2,1)}), bf16[10,2048,512]{1,2,0:T(8,128)(2,1)}) %all-gather.8.cloned.1.call-update) | async-done | bytes 20971536 | tf_op jit(solution)/shard_map/all_gather | solution.py:105
  578.6 12.1 %convert_bitcast_fusion = bf16[10,256,512]{1,2,0:T(8,128)(2,1)} fusion(bf16[10,2048,512]{1,2,0:T(8,128)(2,1)} %all-gather.8.cloned.1.call-done, bf16[256,2048]{1,0:T(8,128)(2,1)S(1)} %copy-done.16), kind=kOutput, calls=%fused_computation.25 | convolution fusion | flops 5370019840 | bytes 24641536 | tf_op jit(solution)/shard_map/yj,zji->zyi/dot_general | solution.py:102
  590.7 1.2 collective-permute-start
  592.2 57.1 %collective-permute-done = bf16[10,256,512]{1,2,0:T(8,128)(2,1)} collective-permute-done((bf16[10,256,512]{1,2,0:T(8,128)(2,1)}, bf16[10,256,512]{1,2,0:T(8,128)(2,1)}, u32[]{:S(2)}, u32[]{:S(2)}) %collective-permute-start) | collective-permute-done | bytes 2621472 | tf_op jit(solution)/shard_map/ppermute | solution.py:15
  649.3 2.1 collective-permute-start.2
  652.0 8.6 select_bitcast_fusion
  660.6 9.8 %slice_convert_fusion.1 = (f32[1,10,256,512]{3,2,1,0:T(8,128)}, f32[1,10,256,512]{3,2,1,0:T(8,128)}) fusion(s32[2,10,256,512]{3,2,1,0:T(8,128)} %param.22), kind=kLoop, calls=%fused_computation.23 | loop fusion | flops 2621440 | bytes 20971520 | tf_op jit(solution)/shard_map/convert_element_type | solution.py:118
  670.5 4.6 copy.18
  675.1 5.4 broadcast_in_dim.47
  680.4 1.8 constant_dynamic-update-slice_fusion.3
  682.3 4.4 copy.19
  686.7 19.6 %collective-permute-done.1 = bf16[10,256,512]{1,2,0:T(8,128)(2,1)} collective-permute-done((bf16[10,256,512]{1,2,0:T(8,128)(2,1)}, bf16[10,256,512]{1,2,0:T(8,128)(2,1)}, u32[]{:S(2)}, u32[]{:S(2)}) %collective-permute-start.1) | collective-permute-done | bytes 2621472 | tf_op jit(solution)/shard_map/ppermute | solution.py:18
  706.3 4.4 copy.20
  710.7 3.7 constant_dynamic-update-slice_fusion.2
  714.4 1.8 constant_dynamic-update-slice_fusion.1
  716.2 45.4 %collective-permute-done.2 = bf16[10,256,512]{1,2,0:T(8,128)(2,1)} collective-permute-done((bf16[10,256,512]{1,2,0:T(8,128)(2,1)}, bf16[10,256,512]{1,2,0:T(8,128)(2,1)}, u32[]{:S(2)}, u32[]{:S(2)}) %collective-permute-start.2) | collective-permute-done | bytes 2621472 | tf_op jit(solution)/shard_map/ppermute | solution.py:15
  761.6 4.4 copy.21
  766.0 3.7 constant_dynamic-update-slice_fusion
  769.7 9.1 %fusion.5 = f32[10,256,512]{2,1,0:T(8,128)S(1)} fusion(bf16[10,256,2048]{2,1,0:T(8,128)(2,1)} %constant_dynamic-update-slice_fusion, bf16[2048,512]{1,0:T(8,128)(2,1)S(1)} %copy-done.14), kind=kOutput, calls=%fused_computation.37 | convolution fusion | flops 5368709120 | bytes 17825792 | tf_op jit(solution)/shard_map/zyi,ix->zyx/dot_general | solution.py:109
  778.9 5.9 pad_maximum_fusion.4
  784.9 3.3 copy.22
  788.2 4.0 collective-permute-start.3
  792.2 3.3 copy.23
  795.5 1.9 collective-permute-start.4
  797.5 3.2 copy.24
  801.1 3.1 copy.25
  804.2 2.3 pad_maximum_fusion.10
  806.6 3.2 collective-permute-start.5
  809.7 3.1 collective-permute-start.6
  812.8 2.9 collective-permute-done.6
  815.7 27.8 %pad_maximum_fusion = f32[4,10,258,514]{3,2,1,0:T(8,128)} fusion(f32[4,10,1,514]{3,2,1,0:T(1,128)S(1)} %collective-permute-done.6, f32[4,10,256,1]{3,2,1,0:T(8,128)S(1)} %copy-done.5, f32[1,10,256,512]{3,2,1,0:T(8,128)} %get-tuple-element.19, f32[1,10,256,512]{3,2,1,0:T(8,128)S(1)} %bitcast.59, f32[1,10,256,512]{3,2,1,0:T(8,128)} %select_bitcast_fusion, ...), kind=kLoop, calls=%fused_computation | loop fusion | flops 37131360 | bytes 42435840 | tf_op jit(solution)/shard_map/concatenate | solution.py:34
  843.6 18.6 %slice_bitcast_fusion.3 = (f32[10,258,514]{2,1,0:T(8,128)}, f32[10,258,514]{2,1,0:T(8,128)}, f32[10,258,514]{2,1,0:T(8,128)}, f32[10,258,514]{2,1,0:T(8,128)}) fusion(f32[4,10,258,514]{3,2,1,0:T(8,128)} %pad_maximum_fusion), kind=kLoop, calls=%fused_computation.4 | loop fusion | bytes 42435840 | tf_op jit(solution)/shard_map/squeeze | solution.py:125
  862.1 15.1 %fusion.1 = f32[10,256,513]{2,1,0:T(8,128)} fusion(f32[10,258,514]{2,1,0:T(8,128)} %get-tuple-element.14, f32[10,258,514]{2,1,0:T(8,128)} %get-tuple-element.15, f32[10,258,514]{2,1,0:T(8,128)} %get-tuple-element.12, pred[513]{0:T(1024)(128)(4,1)S(1)} %fusion.62), kind=kLoop, calls=%fused_computation.7 | loop fusion | flops 6566400 | bytes 31519232 | tf_op jit(solution)/shard_map/jit(_where)/select_n | solution.py:130
  877.2 1.8 copy-done.3
  879.0 10.7 %fusion.3 = f32[10,257,512]{2,1,0:T(8,128)} fusion(f32[10,258,514]{2,1,0:T(8,128)S(1)} %copy-done.2, f32[10,258,514]{2,1,0:T(8,128)S(1)} %copy-done.3, f32[10,258,514]{2,1,0:T(8,128)} %get-tuple-element.13, pred[257]{0:T(512)(128)(4,1)S(1)} %fusion.65), kind=kLoop, calls=%fused_computation.12 | loop fusion | flops 6579200 | bytes 31580416 | tf_op jit(solution)/shard_map/jit(_where)/select_n | solution.py:139
  889.7 11.2 %fusion.4 = f32[10,256,512]{2,1,0:T(8,128)} fusion(f32[10,257,512]{2,1,0:T(8,128)} %fusion.3, f32[10,256,513]{2,1,0:T(8,128)} %fusion.1), kind=kLoop, calls=%fused_computation.16 | loop fusion | flops 3932160 | bytes 26214400 | tf_op jit(solution)/shard_map/add | solution.py:141
  (71 shorter events, 5.6 us)
Async XLA Ops:
  7.2 110.8 %copy-start = (bf16[2048,512]{1,0:T(8,128)(2,1)S(1)}, bf16[2048,512]{1,0:T(8,128)(2,1)}, u32[]{:S(2)}) copy-start(bf16[2048,512]{1,0:T(8,128)(2,1)} %param.17) | copy-start | bytes 6291460
  7.2 110.8 %all-gather.4.cloned.1.call-start = ((), (), s32[]{:S(2)}) async-start(), calls=%async_computation | async-start | bytes 13107200 | tf_op jit(solution)/shard_map/all_gather | solution.py:84
  11.7 116.1 %copy-start.11 = (f32[9]{0:T(128)S(1)}, f32[9]{0:T(128)}, u32[]{:S(2)}) copy-start(f32[9]{0:T(128)} %param.15) | copy-start | bytes 112
  11.7 122.5 %copy-start.10 = (f32[10]{0:T(128)S(1)}, f32[10]{0:T(128)}, u32[]{:S(2)}) copy-start(f32[10]{0:T(128)} %param.16) | copy-start | bytes 124
  11.8 302.8 %copy-start.15 = (bf16[256,2048]{1,0:T(8,128)(2,1)S(1)}, bf16[256,2048]{1,0:T(8,128)(2,1)}, u32[]{:S(2)}) copy-start(bf16[256,2048]{1,0:T(8,128)(2,1)} %param.18) | copy-start | bytes 3145732
  11.8 302.8 %all-gather.6.cloned.1.call-start = ((), (), s32[]{:S(2)}) async-start(), calls=%async_computation.1 | async-start | bytes 23592960 | tf_op jit(solution)/shard_map/all_gather | solution.py:92
  127.5 451.1 %all-gather.8.cloned.1.call-start = ((), (), s32[]{:S(2)}) async-start(), calls=%async_computation.2 | async-start | bytes 23592960 | tf_op jit(solution)/shard_map/all_gather | solution.py:105
  134.9 190.0 %copy-start.9 = (f32[512]{0:T(512)S(1)}, f32[512]{0:T(512)}, u32[]{:S(2)}) copy-start(f32[512]{0:T(512)} %param.13) | copy-start | bytes 6148
  134.9 190.0 %copy-start.12 = (f32[256]{0:T(256)S(1)}, f32[256]{0:T(256)}, u32[]{:S(2)}) copy-start(f32[256]{0:T(256)} %param.14) | copy-start | bytes 3076
  353.9 224.7 %copy-start.16 = (bf16[256,2048]{1,0:T(8,128)(2,1)S(1)}, bf16[256,2048]{1,0:T(8,128)(2,1)}, u32[]{:S(2)}) copy-start(bf16[256,2048]{1,0:T(8,128)(2,1)} %param.19) | copy-start | bytes 3145732
  393.8 257.6 %copy-start.13 = (f32[4]{0:T(128)S(1)}, f32[4]{0:T(128)}, u32[]{:S(2)}) copy-start(f32[4]{0:T(128)} %param.23) | copy-start | bytes 52
  590.7 58.5 %collective-permute-start = (bf16[10,256,512]{1,2,0:T(8,128)(2,1)}, bf16[10,256,512]{1,2,0:T(8,128)(2,1)}, u32[]{:S(2)}, u32[]{:S(2)}) collective-permute-start(bf16[10,256,512]{1,2,0:T(8,128)(2,1)} %convert_bitcast_fusion), channel_id=1, source_target_pairs={{0,8},{8,16},{16,24},{24,0},{1,9},{9,17},{17,25},{25,1},{2,10},{10... | collective-permute-start | bytes 7864328 | tf_op jit(solution)/shard_map/ppermute | solution.py:15
  591.9 114.4 %collective-permute-start.1 = (bf16[10,256,512]{1,2,0:T(8,128)(2,1)}, bf16[10,256,512]{1,2,0:T(8,128)(2,1)}, u32[]{:S(2)}, u32[]{:S(2)}) collective-permute-start(bf16[10,256,512]{1,2,0:T(8,128)(2,1)} %convert_bitcast_fusion), channel_id=1, source_target_pairs={{0,24},{8,0},{16,8},{24,16},{1,25},{9,1},{17,9},{25,17},{2,26},{10... | collective-permute-start | bytes 7864328 | tf_op jit(solution)/shard_map/ppermute | solution.py:18
  649.3 112.4 %collective-permute-start.2 = (bf16[10,256,512]{1,2,0:T(8,128)(2,1)}, bf16[10,256,512]{1,2,0:T(8,128)(2,1)}, u32[]{:S(2)}, u32[]{:S(2)}) collective-permute-start(bf16[10,256,512]{1,2,0:T(8,128)(2,1)} %collective-permute-done), channel_id=1, source_target_pairs={{0,8},{8,16},{16,24},{24,0},{1,9},{9,17},{17,25},{25,1},{2,10},{10... | collective-permute-start | bytes 7864328 | tf_op jit(solution)/shard_map/ppermute | solution.py:15
  675.1 5.4 copy-start.8
  710.7 3.7 copy-start.7
  716.2 53.5 %copy-start.14 = (bf16[2048,512]{1,0:T(8,128)(2,1)S(1)}, bf16[2048,512]{1,0:T(8,128)(2,1)}, u32[]{:S(2)}) copy-start(bf16[2048,512]{1,0:T(8,128)(2,1)} %param.20) | copy-start | bytes 6291460
  766.0 12.9 %slice-start = ((s8[5242880]{0:T(1024)(128)(4,1)}), s8[4194304]{0:T(1024)(128)(4,1)S(1)}, s32[]{:S(2)}) async-start(s8[5242880]{0:T(1024)(128)(4,1)} %bitcast.56), calls=%async_computation.3 | async-start | bytes 8388608
  766.0 12.9 %slice-start.4 = ((s8[5242880]{0:T(1024)(128)(4,1)}), s8[4194304]{0:T(1024)(128)(4,1)S(1)}, s32[]{:S(2)}) async-start(s8[5242880]{0:T(1024)(128)(4,1)} %bitcast.60), calls=%async_computation.7 | async-start | bytes 8388608
  766.0 12.9 %slice-start.6 = ((s8[5242880]{0:T(1024)(128)(4,1)}), s8[4194304]{0:T(1024)(128)(4,1)S(1)}, s32[]{:S(2)}) async-start(s8[5242880]{0:T(1024)(128)(4,1)} %bitcast.62), calls=%async_computation.9 | async-start | bytes 8388608
  769.7 9.2 %slice-start.1 = ((s8[5242880]{0:T(1024)(128)(4,1)}), s8[1048576]{0:T(1024)(128)(4,1)S(1)}, s32[]{:S(2)}) async-start(s8[5242880]{0:T(1024)(128)(4,1)} %bitcast.56), calls=%async_computation.4 | async-start | bytes 2097152
  769.7 9.2 %slice-start.5 = ((s8[5242880]{0:T(1024)(128)(4,1)}), s8[1048576]{0:T(1024)(128)(4,1)S(1)}, s32[]{:S(2)}) async-start(s8[5242880]{0:T(1024)(128)(4,1)} %bitcast.60), calls=%async_computation.8 | async-start | bytes 2097152
  769.7 9.2 %slice-start.7 = ((s8[5242880]{0:T(1024)(128)(4,1)}), s8[1048576]{0:T(1024)(128)(4,1)S(1)}, s32[]{:S(2)}) async-start(s8[5242880]{0:T(1024)(128)(4,1)} %bitcast.62), calls=%async_computation.10 | async-start | bytes 2097152
  778.8 6.0 copy-start.6
  788.2 9.3 %collective-permute-start.3 = (f32[4,10,256,1]{2,0,3,1:T(4,128)S(1)}, f32[4,10,256,1]{2,0,3,1:T(4,128)S(1)}, u32[]{:S(2)}, u32[]{:S(2)}) collective-permute-start(f32[4,10,256,1]{2,0,3,1:T(4,128)S(1)} %copy.22), channel_id=1, source_target_pairs={{0,8},{8,16},{16,24},{1,9},{9,17},{17,25},{2,10},{10,18},{18,26},{... | collective-permute-start | bytes 122888 | tf_op jit(solution)/shard_map/ppermute | solution.py:30
  795.5 5.6 collective-permute-start.4
  801.1 14.6 %slice-start.2 = ((s8[5242880]{0:T(1024)(128)(4,1)}), s8[1048576]{0:T(1024)(128)(4,1)S(1)}, s32[]{:S(2)}) async-start(s8[5242880]{0:T(1024)(128)(4,1)} %bitcast.58), calls=%async_computation.5 | async-start | bytes 2097152
  804.2 11.5 %slice-start.3 = ((s8[5242880]{0:T(1024)(128)(4,1)}), s8[4194304]{0:T(1024)(128)(4,1)S(1)}, s32[]{:S(2)}) async-start(s8[5242880]{0:T(1024)(128)(4,1)} %bitcast.58), calls=%async_computation.6 | async-start | bytes 8388608
  804.2 11.5 %copy-start.4 = (f32[4,10,256,1]{3,2,1,0:T(8,128)S(1)}, f32[4,10,256,1]{3,2,1,0:T(8,128)}, u32[]{:S(2)}) copy-start(f32[4,10,256,1]{3,2,1,0:T(8,128)} %copy.24) | copy-start | bytes 122884
  804.2 11.5 %copy-start.5 = (f32[4,10,256,1]{3,2,1,0:T(8,128)S(1)}, f32[4,10,256,1]{3,2,1,0:T(8,128)}, u32[]{:S(2)}) copy-start(f32[4,10,256,1]{3,2,1,0:T(8,128)} %copy.25) | copy-start | bytes 122884
  806.6 6.3 collective-permute-start.5
  809.7 6.0 collective-permute-start.6
  862.1 15.1 %copy-start.2 = (f32[10,258,514]{2,1,0:T(8,128)S(1)}, f32[10,258,514]{2,1,0:T(8,128)}, u32[]{:S(2)}) copy-start(f32[10,258,514]{2,1,0:T(8,128)} %get-tuple-element.14) | copy-start | bytes 15913444
  862.1 16.9 %copy-start.3 = (f32[10,258,514]{2,1,0:T(8,128)S(1)}, f32[10,258,514]{2,1,0:T(8,128)}, u32[]{:S(2)}) copy-start(f32[10,258,514]{2,1,0:T(8,128)} %get-tuple-element.15) | copy-start | bytes 15913444
  889.7 11.2 %copy-start.1 = (bf16[2048,512]{1,0:T(8,128)(2,1)S(1)}, bf16[2048,512]{1,0:T(8,128)(2,1)}, u32[]{:S(2)}) copy-start(bf16[2048,512]{1,0:T(8,128)(2,1)} %param.17) | copy-start | bytes 6291460
Sparse Core Ops, SparseCore 0:
  11.9 106.1 all-gather.3
  127.6 186.9 all-gather.5
  393.9 184.6 all-gather.7
